TPU v7x, 128 devices: a whole 4x4x4 slice. The times are simulated.
128 devices in a mesh: req: 32 (over x, y, core), tp: 4 (over z).
Axes of the slice: x: 4, y: 4, z: 4, core: 2. Of those that a mesh axis runs over, the one named last changes fastest.
Arguments:
- stream: bfloat16 [64, 64, 3584], P('req'), may hold values from -40 to 40
- queries: bfloat16 [64, 64, 3584], P('req', None, 'tp'), may hold values from -4 to 4
- key_new: bfloat16 [64, 64, 3584], P('req', None, 'tp'), may hold values from -18 to 18
- value_new: bfloat16 [64, 64, 3584], P('req', None, 'tp'), may hold values from -6 to 6
- cache_key: bfloat16 [64, 1024, 3584], P('req', None, 'tp'), may hold values from -5 to 5
- cache_value: bfloat16 [64, 1024, 3584], P('req', None, 'tp'), may hold values from -6 to 6
- cache_length: int32 [64], P('req'), may hold values from 64 to 1024, as said below
- parents: int32 [64, 64], P('req'), may hold values from -1 to 62, as said below
- accept: int32 [64, 8, 64], P('req'), may hold values from 0 to 1, as said below
- out_weight: bfloat16 [3584, 3584], P('tp'), may hold values from -0.75 to 0.75
- norm_gain: float32 [3584], replicated, may hold values from 0.1 to 1.9
- head_weight: bfloat16 [32000, 3584], P('req'), may hold values from -1 to 1
- candidate: int32 [64, 64], replicated, may hold values from 0 to 31999
- dealing: int32 [64], replicated, may hold values from 0 to 63, each once
Outputs:
- target_logprob: float32 [64, 64], P('req')
- accepted_state: bfloat16 [64, 8, 3584], P('req', None, 'tp')
Inputs may be any that keep to these rules, and one draw needn't show every extreme that they name: `cache_length`: every cache holds at least 64 live positions; in every draw some slot's cache is full. `parents`: node 0 is the root with parent -1; node t > 0 lies at depth (t - 1) // 9 + 1 and its parent lies one depth above it. `accept`: row a of a slot's matrix is one-hot on the node at depth a of the accepted path, which runs from the root down the slot's tree to some node; rows past the path's end are zero; in every draw some path ends at the deepest level.
All inputs are finite; a program needn't handle non-finite values.
Results may differ from a plain program's by a relative error of at most 0.012.
Values may be sent and summed in bfloat16 or wider, within the bound.
No kernel may reach another device: no remote copies, remote signals or barrier semaphores. Data moves between devices by JAX's collectives and lax.ppermute only.
A program may use at most 192 MiB of HBM per device.

v0:
```python
import jax
import jax.numpy as jnp
from jax import lax
from jax.sharding import PartitionSpec as P

HD = 224
ACC = 8
EPS = 1e-05
HIGH = lax.Precision.HIGHEST
block_limit = 512


def combined_all(value, axis, join):
    pieces = jax.tree.map(lambda part: lax.all_gather(part, axis), value)
    head = jax.tree.map(lambda part: part[0], pieces)
    tail = jax.tree.map(lambda part: part[1:], pieces)
    subtotal, _ = lax.scan(lambda subtotal, share: (join(subtotal, share), None), head, tail)
    return subtotal


def ancestry(parents):
    node_count = parents.shape[-1]
    node_ids = jnp.arange(node_count, dtype=jnp.int32)
    stride_map = (parents[..., :, None] == node_ids).astype(jnp.float32)
    reached = jnp.broadcast_to(jnp.eye(node_count, dtype=jnp.float32), stride_map.shape) > 0.5
    for doubling in range((ACC - 1).bit_length()):
        further = lax.optimization_barrier(
            jnp.einsum("rtk,rku->rtu", reached.astype(jnp.float32), stride_map, precision=HIGH)
        )
        reached = jnp.logical_or(reached, further > 0.5)
        stride_map = jnp.einsum("rtk,rku->rtu", stride_map, stride_map, precision=HIGH)
    return reached


def combine_stats(earlier, later):
    joint_max = jnp.maximum(earlier[0], later[0])
    joint_sum = earlier[1] * jnp.exp(earlier[0] - joint_max) + later[1] * jnp.exp(
        later[0] - joint_max
    )
    return (joint_max, joint_sum, earlier[2] + later[2])


def vocab_stats(logits, vocab_ids, wanted, along):
    row_max = jnp.max(logits, axis=along)
    row_sum = jnp.sum(jnp.exp(logits - jnp.expand_dims(row_max, along)), axis=along)
    matches = jnp.expand_dims(vocab_ids, 1 - along) == jnp.expand_dims(wanted, along)
    picked = jnp.sum(jnp.where(matches, logits, 0.0), axis=along)
    return (row_max, row_sum, picked)


def local(
    stream,
    queries,
    key_new,
    value_new,
    cache_key,
    cache_value,
    cache_length,
    parents,
    accept,
    out_weight,
    norm_gain,
    head_weight,
    candidate,
    dealing,
):
    slots, tree_size, qwidth = queries.shape
    model_width = stream.shape[2]
    heads_loc = qwidth // HD
    n_tp = lax.axis_size("tp")
    n_req = lax.axis_size("req")
    tp_id = lax.axis_index("tp")
    req_id = lax.axis_index("req")
    score_scale = HD ** (-0.5)
    query_rows = queries.reshape(slots, tree_size, heads_loc, HD)
    tree_keys = key_new.reshape(slots, tree_size, heads_loc, HD)
    tree_values = value_new.reshape(slots, tree_size, heads_loc, HD)
    visible = ancestry(parents)
    tree_scores = (
        jnp.einsum("rthd,rkhd->rhtk", query_rows, tree_keys, preferred_element_type=jnp.float32)
        * score_scale
    )
    tree_scores = jnp.where(visible[:, None], tree_scores, -jnp.inf)
    running_max = jnp.max(tree_scores, axis=3)
    weights = jnp.exp(tree_scores - running_max[..., None])
    running_sum = jnp.sum(weights, axis=3)
    running_out = jnp.einsum(
        "rhtk,rkhd->rhtd",
        weights.astype(jnp.bfloat16),
        tree_values,
        preferred_element_type=jnp.float32,
    )
    cache_cap = cache_key.shape[1]
    block_rows = min(block_limit, cache_cap)
    block_count = (jnp.max(cache_length) + block_rows - 1) // block_rows

    def visit_block(block_index, folded):
        old_max, old_sum, old_out = folded
        offset = block_index * block_rows
        past_keys = lax.dynamic_slice_in_dim(cache_key, offset, block_rows, 1).reshape(
            slots, block_rows, heads_loc, HD
        )
        past_values = lax.dynamic_slice_in_dim(cache_value, offset, block_rows, 1).reshape(
            slots, block_rows, heads_loc, HD
        )
        scores = (
            jnp.einsum("rthd,rkhd->rhtk", query_rows, past_keys, preferred_element_type=jnp.float32)
            * score_scale
        )
        live_mask = (offset + jnp.arange(block_rows, dtype=jnp.int32))[None, :] < cache_length[
            :, None
        ]
        scores = jnp.where(live_mask[:, None, None, :], scores, -jnp.inf)
        new_max = jnp.maximum(old_max, jnp.max(scores, axis=3))
        shrink = jnp.exp(old_max - new_max)
        block_weights = jnp.exp(scores - new_max[..., None])
        new_sum = old_sum * shrink + jnp.sum(block_weights, axis=3)
        contribution = lax.optimization_barrier(
            jnp.einsum(
                "rhtk,rkhd->rhtd",
                block_weights.astype(jnp.bfloat16),
                past_values,
                preferred_element_type=jnp.float32,
            )
        )
        new_out = old_out * shrink[..., None] + contribution
        return (new_max, new_sum, new_out)

    running_max, running_sum, running_out = lax.fori_loop(
        0, block_count, visit_block, (running_max, running_sum, running_out)
    )
    attention = (running_out / running_sum[..., None]).astype(jnp.bfloat16)
    attention_rows = attention.transpose(0, 2, 1, 3).reshape(slots * tree_size, qwidth)
    flat_stream = stream.reshape(slots * tree_size, model_width)
    rows_all = slots * tree_size
    quarter = rows_all // n_tp
    dslice = model_width // n_tp
    partial_out = jnp.dot(attention_rows, out_weight, preferred_element_type=jnp.float32)
    summed = lax.psum_scatter(
        partial_out.astype(jnp.bfloat16), "tp", scatter_dimension=1, tiled=True
    ).astype(jnp.float32)
    own_stream = lax.dynamic_slice_in_dim(flat_stream, tp_id * dslice, dslice, 1)
    post_rows = (own_stream.astype(jnp.float32) + summed).astype(jnp.bfloat16)
    post_float = post_rows.astype(jnp.float32)
    square = jnp.sum(post_float * post_float, axis=1)
    energy = lax.psum(square, "tp")
    inverse = lax.rsqrt(energy / model_width + EPS)
    part_gain = lax.dynamic_slice_in_dim(norm_gain, tp_id * dslice, dslice, 0)
    normed_slice = (post_float * inverse[:, None] * part_gain[None, :]).astype(jnp.bfloat16)
    compact = jnp.einsum(
        "sat,std->sad",
        accept.astype(jnp.bfloat16),
        post_rows.reshape(slots, tree_size, dslice),
        preferred_element_type=jnp.float32,
    ).astype(jnp.bfloat16)
    normed = lax.all_to_all(normed_slice, "tp", split_axis=0, concat_axis=1, tiled=True)
    vocab_loc = head_weight.shape[0]
    wanted_rows = lax.dynamic_slice_in_dim(
        candidate.reshape(n_req, rows_all), tp_id * quarter, quarter, 1
    ).reshape(-1)
    vocab_ids = req_id * vocab_loc + jnp.arange(vocab_loc, dtype=jnp.int32)
    logits = lax.dot_general(
        lax.all_gather(normed, "req", axis=0, tiled=True),
        head_weight,
        (((1,), (1,)), ((), ())),
        preferred_element_type=jnp.float32,
    )
    found_stats = vocab_stats(logits, vocab_ids, wanted_rows, 1)
    local_stats = tuple((after_part for after_part in found_stats))
    merged = combined_all((local_stats[0], local_stats[1], local_stats[2]), "req", combine_stats)
    all_stats = (
        lax.all_gather(merged[0], "tp", axis=0, tiled=True),
        lax.all_gather(merged[1], "tp", axis=0, tiled=True),
        lax.all_gather(merged[2], "tp", axis=0, tiled=True),
    )
    row_max, row_sum, picked = tuple(
        (
            member.reshape(n_tp, n_req, quarter).transpose(1, 0, 2).reshape(-1)
            for member in all_stats
        )
    )
    logprob = (picked - row_max - jnp.log(row_sum)).reshape(-1, tree_size)
    own_requests = req_id * slots + jnp.arange(slots, dtype=jnp.int32)
    selector = dealing[None, :] == own_requests[:, None]
    target_logprob = jnp.dot(selector.astype(jnp.float32), logprob, precision=HIGH)
    home_states = lax.all_gather(compact, "req", axis=0, tiled=True)
    accepted_state = jnp.einsum(
        "ks,sad->kad",
        selector.astype(jnp.bfloat16),
        home_states,
        preferred_element_type=jnp.float32,
    ).astype(jnp.bfloat16)
    return (target_logprob, accepted_state)


def solution(mesh):
    placed = (
        P("req", None, None),
        P("req", None, "tp"),
        P("req", None, "tp"),
        P("req", None, "tp"),
        P("req", None, "tp"),
        P("req", None, "tp"),
        P("req"),
        P("req", None),
        P("req", None, None),
        P("tp", None),
        P(),
        P("req", None),
        P(),
        P(),
    )
    return jax.shard_map(
        local,
        mesh=mesh,
        in_specs=placed,
        out_specs=(P("req", None), P("req", None, "tp")),
        check_vma=False,
    )
```

profile of v0, /device:TPU:0, one launch (start us, length us, event | category | flops | bytes accessed | tf_op | source)
XLA Modules:
  0.0 275.6 jit_solution(6451548967636028759)
XLA Ops:
  7.2 1.4 reduce_max.37
  11.9 1.2 reshape.97
  15.1 1.2 reshape.99
  16.9 12.5 %while.28 = (s32[]{:T(128)}, f32[2,4,64]{2,1,0:T(4,128)S(1)}, f32[2,4,64]{2,1,0:T(4,128)S(1)}, f32[2,4,64,224]{3,2,1,0:T(8,128)S(1)}, s32[]{:T(128)}, /*index=5*...) while((s32[]{:T(128)}, f32[2,4,64]{2,1,0:T(4,128)S(1)}, ...), condition=%wide.region_6.7_spmd, body=%wide.region_3.6_spmd.sunk | while | flops 236947968 | bytes 23599292 | solution.py:129
  17.0 4.1 %constant_dynamic-slice_fusion.9 = (bf16[2,512,896]{2,1,0:T(8,128)(2,1)}, bf16[2,512,896]{2,1,0:T(8,128)(2,1)}) fusion(bf16[2,1024,896]{2,1,0:T(8,128)(2,1)} %get-tuple-element.346, s32[]{:T(128)S(6)} %select_n.42, bf16[2,1024,896]{2,1,0:T(8,128)(2,1)} %get-tuple-element.344), kind=kLoop, calls=%fused_computation.13.clone.1 | loop fusion | bytes 7340036 | tf_op jit(solution)/shard_map/while/body/dynamic_slice | solution.py:103
  21.1 2.7 copy.80
  23.9 1.5 fusion.66
  25.8 2.8 copy.81
  30.0 4.0 %convolution_convert_fusion = bf16[128,3584]{1,0:T(8,128)(2,1)S(1)} fusion(bf16[128,896]{1,0:T(8,128)(2,1)S(1)} %reshape.100, bf16[896,3584]{1,0:T(8,128)(2,1)} %param.27), kind=kOutput, calls=%fused_computation.19 | convolution fusion | flops 822542336 | bytes 7569408 | tf_op jit(solution)/shard_map/dot_general | solution.py:138
  34.0 1.3 copy.61
  36.1 37.4 %reduce-scatter.4.cloned.1.call-done = bf16[896,128]{1,0:T(8,128)(2,1)} async-done(((bf16[3584,128]{1,0:T(8,128)(2,1)}), bf16[896,128]{1,0:T(8,128)(2,1)}) %reduce-scatter.4.cloned.1.call-update) | async-done | bytes 229392
  75.7 8.0 %psum.7 = f32[128]{0:T(128)S(1)} all-reduce(f32[128]{0:T(128)S(1)} %get-tuple-element.177), channel_id=1, replica_groups=mesh['req'=32,'tp'=4] {'tp'}, use_global_device_ids=true, to_apply=%region_9.10 | all-reduce | flops 128 | bytes 1024 | tf_op jit(solution)/shard_map/psum | solution.py:146
  83.9 9.3 %all_to_all.19 = bf16[4,32,896]{2,1,0:T(8,128)(2,1)S(1)} all-to-all(bf16[4,32,896]{2,1,0:T(8,128)(2,1)S(1)} %bitcast.79), channel_id=1, replica_groups=mesh['req'=32,'tp'=4] {'tp'}, dimensions={0} | all-to-all | bytes 458752 | tf_op jit(solution)/shard_map/all_to_all | solution.py:156
  94.3 25.4 %all_gather.43 = bf16[64,8,896]{2,1,0:T(8,128)(2,1)S(1)} all-gather(bf16[2,8,896]{2,1,0:T(8,128)(2,1)S(1)} %fusion.8), channel_id=1, replica_groups=mesh['req'=32,'tp'=4] {'req'}, dimensions={0}, use_global_device_ids=true | all-gather | bytes 946176 | tf_op jit(solution)/shard_map/all_gather | solution.py:186
  120.7 23.6 %all-gather.5.cloned.1.call-done = bf16[1024,3584]{1,0:T(8,128)(2,1)} async-done(((bf16[32,3584]{1,0:T(8,128)(2,1)}), bf16[1024,3584]{1,0:T(8,128)(2,1)}) %all-gather.5.cloned.1.call-update) | async-done | bytes 7340048 | tf_op jit(solution)/shard_map/all_gather | solution.py:163
  144.2 12.1 %fusion.36 = (f32[1024]{0:T(1024)S(1)}, f32[1024,1000]{0,1:T(8,128)S(1)}) fusion(bf16[1024,3584]{1,0:T(8,128)(2,1)} %all-gather.5.cloned.1.call-done, bf16[1000,3584]{1,0:T(8,128)(2,1)} %param.29), kind=kOutput, calls=%fused_computation.70 | convolution fusion | flops 7341054976 | bytes 18608128 | tf_op jit(solution)/shard_map/dot_general | solution.py:162
  156.3 1.4 select_reduce_fusion
  157.7 24.1 %all-gather.2 = f32[32768]{0:T(1024)S(1)} all-gather(f32[1024]{0:T(1024)S(1)} %get-tuple-element.139), channel_id=4, replica_groups=mesh['req'=32,'tp'=4] {'req'}, dimensions={0}, use_global_device_ids=true | all-gather | bytes 135168 | tf_op jit(solution)/shard_map/all_gather | solution.py:14
  181.8 22.7 %all-gather = f32[32768]{0:T(1024)S(1)} all-gather(f32[1024]{0:T(1024)S(1)} %get-tuple-element.187), channel_id=2, replica_groups=mesh['req'=32,'tp'=4] {'req'}, dimensions={0}, use_global_device_ids=true | all-gather | bytes 135168 | tf_op jit(solution)/shard_map/all_gather | solution.py:14
  204.5 23.8 %all-gather.1 = f32[32768]{0:T(1024)S(1)} all-gather(f32[1024]{0:T(1024)S(1)} %get-tuple-element.140), channel_id=3, replica_groups=mesh['req'=32,'tp'=4] {'req'}, dimensions={0}, use_global_device_ids=true | all-gather | bytes 135168 | tf_op jit(solution)/shard_map/all_gather | solution.py:14
  228.4 2.8 %while.29 = (s32[]{:T(128)}, f32[1024]{0:T(1024)S(1)}, f32[1024]{0:T(1024)S(1)}, f32[1024]{0:T(1024)S(1)}, f32[31,1024]{1,0:T(8,128)S(1)}, /*index=5*/f32[31,1024]{1,0:T(8,128)S(1)}, f32[31,1024]{1,0:T(8,128)S(1)}, s32[]{:T(128)}) while((s32[]{:T(128)}, f32[1024]{0:T(1024)S(1)}, f32[1024]{0:T(1024)S(1)}, f32[1024]{0:T(1024)S(1)}, ...), condition=%wide.region_14.15_spmd, body=%wide.region_13.14_spmd.sunk | while | flops 7170 | bytes 61541 | solution.py:17
  231.2 12.5 %all_gather.40 = f32[4096]{0:T(1024)S(1)} all-gather(f32[1024]{0:T(1024)S(1)} %get-tuple-element.92), channel_id=1, replica_groups=mesh['req'=32,'tp'=4] {'tp'}, dimensions={0}, use_global_device_ids=true | all-gather | bytes 20480 | tf_op jit(solution)/shard_map/all_gather | solution.py:174
  243.7 12.0 %all_gather.41 = f32[4096]{0:T(1024)S(1)} all-gather(f32[1024]{0:T(1024)S(1)} %get-tuple-element.93), channel_id=1, replica_groups=mesh['req'=32,'tp'=4] {'tp'}, dimensions={0}, use_global_device_ids=true | all-gather | bytes 20480 | tf_op jit(solution)/shard_map/all_gather | solution.py:172
  255.7 12.0 %all_gather.42 = f32[4096]{0:T(1024)S(1)} all-gather(f32[1024]{0:T(1024)S(1)} %get-tuple-element.94), channel_id=1, replica_groups=mesh['req'=32,'tp'=4] {'tp'}, dimensions={0}, use_global_device_ids=true | all-gather | bytes 20480 | tf_op jit(solution)/shard_map/all_gather | solution.py:173
  (189 shorter events, 14.7 us)
Async XLA Ops:
  7.2 9.7 %copy-start.1 = (s32[2]{0:T(128)S(1)}, s32[2]{0:T(128)}, u32[]{:S(2)}) copy-start(s32[2]{0:T(128)} %param.24) | copy-start | bytes 28
  7.2 66.4 %reduce-scatter.4.cloned.1.call-start = ((), (), s32[]{:S(2)}) async-start(), calls=%async_computation.3 | async-start | bytes 1146880
  34.0 60.0 %copy-start = (s32[64,64]{1,0:T(8,128)S(1)}, s32[64,64]{1,0:T(8,128)}, u32[]{:S(2)}) copy-start(s32[64,64]{1,0:T(8,128)} %param.30) | copy-start | bytes 49156
  34.0 60.2 %copy-start.2 = (s32[2,8,64]{2,1,0:T(8,128)S(1)}, s32[2,8,64]{2,1,0:T(8,128)}, u32[]{:S(2)}) copy-start(s32[2,8,64]{2,1,0:T(8,128)} %param.26) | copy-start | bytes 12292
  34.0 85.8 %copy-start.3 = (s32[64]{0:T(128)S(1)}, s32[64]{0:T(128)}, u32[]{:S(2)}) copy-start(s32[64]{0:T(128)} %param.31) | copy-start | bytes 772
  35.3 108.9 %all-gather.5.cloned.1.call-start = ((), (), s32[]{:S(2)}) async-start(), calls=%async_computation.2 | async-start | bytes 7569408 | tf_op jit(solution)/shard_map/all_gather | solution.py:163
Sparse Core Ops, SparseCore 0:
  35.4 38.0 reduce-scatter.3
  94.1 50.1 all-gather.4
where the time goes:
time: 276 us
  blocking collectives  150 us (54%)
  waiting for transfers between devices  61 us (22%)
  matrix products  22.3 us (8%)
  local copies, waits for them, and re-layouts  20.5 us (7%)
  between operations  15 us (5%)
  other arithmetic  5.41 us (2%)
    all_gather x3, blocking collectives, combined_all(): pieces = jax.tree.map(lambda part: lax.all_gather(part, axis), value)  70.6 us
    unnamed x3, waiting for transfers between devices  37.4 us
    all_gather x1, blocking collectives, local(): home_states = lax.all_gather(compact, 'req', axis=0, tiled=True)  25.4 us
    all_gather x1, waiting for transfers between devices, local(): lax.all_gather(normed, 'req', axis=0, tiled=True)  23.6 us
    all_gather x1, blocking collectives, local(): lax.all_gather(merged[2], 'tp', axis=0, tiled=True)  12.5 us
    dot_general x1, matrix products, local(): lax.dot_general(lax.all_gather(normed, 'req', axis=0, tiled=True), head_w...  12.1 us
    all_gather x1, blocking collectives, local(): lax.all_gather(merged[0], 'tp', axis=0, tiled=True)  12 us
    all_gather x1, blocking collectives, local(): lax.all_gather(merged[1], 'tp', axis=0, tiled=True)  12 us
  transfers between devices with their start and end apart: 2, of which 2 were waited for; matrix products, arithmetic and copies ran while one was open for 1% of the time, Pallas kernels for 0%

commit v1 on v0

--- a/solution.py
+++ b/solution.py
@@ -143,7 +143,19 @@
     post_rows = (own_stream.astype(jnp.float32) + summed).astype(jnp.bfloat16)
     post_float = post_rows.astype(jnp.float32)
     square = jnp.sum(post_float * post_float, axis=1)
-    energy = lax.psum(square, "tp")
+
+    def shelves_push(row_data, mesh_ax):
+        dev_n = lax.axis_size(mesh_ax)
+        known, prior = (row_data, 0)
+        while 1 << prior < dev_n:
+            y2 = lax.ppermute(
+                known, mesh_ax, [(hop_no, hop_no ^ 1 << prior) for hop_no in range(dev_n)]
+            )
+            known = known + y2
+            prior = prior + 1
+        return known
+
+    energy = shelves_push(square, "tp")
     inverse = lax.rsqrt(energy / model_width + EPS)
     part_gain = lax.dynamic_slice_in_dim(norm_gain, tp_id * dslice, dslice, 0)
     normed_slice = (post_float * inverse[:, None] * part_gain[None, :]).astype(jnp.bfloat16)

time: 276 us -> 277 us (level)
  blocking collectives: 150 us -> 142 us
  waiting for transfers between devices: 61 us -> 68.2 us
    psum x1 -> x0, blocking collectives: 7.98 us -> none  [local(): energy = lax.psum(square, 'tp')]
    ppermute x0 -> x2, waiting for transfers between devices: none -> 6.39 us  [shelves_push(): lax.ppermute(known, mesh_ax, [(hop_no, hop_no ^ 1 << prior) for hop_no in...]
  transfers between devices with their start and end apart: 2 -> 4, of which waited for: 2 -> 4; matrix products, arithmetic and copies ran while one was open for 1% -> 1% of each run, Pallas kernels for 0% -> 0%
where the time goes in v1:
time: 277 us; the launch traced here: 276 us
  blocking collectives  142 us (51%)
  waiting for transfers between devices  68.2 us (25%)
  matrix products  22.3 us (8%)
  local copies, waits for them, and re-layouts  20.5 us (7%)
  between operations  15.1 us (5%)
  other arithmetic  5.42 us (2%)
    all_gather x3, blocking collectives, combined_all(): pieces = jax.tree.map(lambda part: lax.all_gather(part, axis), value)  70.6 us
    unnamed x3, waiting for transfers between devices  38.2 us
    all_gather x1, blocking collectives, local(): home_states = lax.all_gather(compact, 'req', axis=0, tiled=True)  25.4 us
    all_gather x1, waiting for transfers between devices, local(): lax.all_gather(normed, 'req', axis=0, tiled=True)  23.6 us
    all_gather x1, blocking collectives, local(): lax.all_gather(merged[2], 'tp', axis=0, tiled=True)  12.5 us
    dot_general x1, matrix products, local(): lax.dot_general(lax.all_gather(normed, 'req', axis=0, tiled=True), head_w...  12.1 us
    all_gather x1, blocking collectives, local(): lax.all_gather(merged[0], 'tp', axis=0, tiled=True)  12 us
    all_gather x1, blocking collectives, local(): lax.all_gather(merged[1], 'tp', axis=0, tiled=True)  12 us
  transfers between devices with their start and end apart: 4, of which 4 were waited for; matrix products, arithmetic and copies ran while one was open for 1% of the time, Pallas kernels for 0%

profile of v1, /device:TPU:0, one launch (start us, length us, event | category | flops | bytes accessed | tf_op | source)
XLA Modules:
  0.0 276.0 jit_solution(9484009583331463496)
XLA Ops:
  7.2 1.4 reduce_max.37
  16.9 12.5 %while.28 = (s32[]{:T(128)}, f32[2,4,64]{2,1,0:T(4,128)S(1)}, f32[2,4,64]{2,1,0:T(4,128)S(1)}, f32[2,4,64,224]{3,2,1,0:T(8,128)S(1)}, s32[]{:T(128)}, /*index=5*...) while((s32[]{:T(128)}, f32[2,4,64]{2,1,0:T(4,128)S(1)}, ...), condition=%wide.region_6.7_spmd, body=%wide.region_3.6_spmd.sunk | while | flops 236947968 | bytes 23599292 | solution.py:129
  17.0 4.1 %constant_dynamic-slice_fusion.9 = (bf16[2,512,896]{2,1,0:T(8,128)(2,1)}, bf16[2,512,896]{2,1,0:T(8,128)(2,1)}) fusion(bf16[2,1024,896]{2,1,0:T(8,128)(2,1)} %get-tuple-element.346, s32[]{:T(128)S(6)} %select_n.42, bf16[2,1024,896]{2,1,0:T(8,128)(2,1)} %get-tuple-element.344), kind=kLoop, calls=%fused_computation.13.clone.1 | loop fusion | bytes 7340036 | tf_op jit(solution)/shard_map/while/body/dynamic_slice | solution.py:103
  21.1 2.7 copy.80
  23.9 1.5 fusion.66
  25.8 2.8 copy.81
  30.0 4.0 %convolution_convert_fusion = bf16[128,3584]{1,0:T(8,128)(2,1)S(1)} fusion(bf16[128,896]{1,0:T(8,128)(2,1)S(1)} %reshape.100, bf16[896,3584]{1,0:T(8,128)(2,1)} %param.27), kind=kOutput, calls=%fused_computation.19 | convolution fusion | flops 822542336 | bytes 7569408 | tf_op jit(solution)/shard_map/dot_general | solution.py:138
  34.0 1.3 copy.61
  35.4 38.2 %reduce-scatter.4.cloned.1.call-done = bf16[896,128]{1,0:T(8,128)(2,1)} async-done(((bf16[3584,128]{1,0:T(8,128)(2,1)}), bf16[896,128]{1,0:T(8,128)(2,1)}) %reduce-scatter.4.cloned.1.call-update) | async-done | bytes 229392
  75.8 3.6 %collective-permute-done = f32[128]{0:T(128)S(1)} collective-permute-done((f32[128]{0:T(128)S(1)}, f32[128]{0:T(128)S(1)}, u32[]{:S(2)}, u32[]{:S(2)}) %collective-permute-start) | collective-permute-done | bytes 544 | tf_op jit(solution)/shard_map/ppermute | solution.py:151
  79.4 1.5 collective-permute-start.1
  81.6 2.8 %collective-permute-done.1 = f32[128]{0:T(128)S(1)} collective-permute-done((f32[128]{0:T(128)S(1)}, f32[128]{0:T(128)S(1)}, u32[]{:S(2)}, u32[]{:S(2)}) %collective-permute-start.1) | collective-permute-done | bytes 544 | tf_op jit(solution)/shard_map/ppermute | solution.py:151
  84.6 9.0 %all_to_all.19 = bf16[4,32,896]{2,1,0:T(8,128)(2,1)S(1)} all-to-all(bf16[4,32,896]{2,1,0:T(8,128)(2,1)S(1)} %bitcast.79), channel_id=1, replica_groups=mesh['req'=32,'tp'=4] {'tp'}, dimensions={0} | all-to-all | bytes 458752 | tf_op jit(solution)/shard_map/all_to_all | solution.py:168
  94.8 25.4 %all_gather.43 = bf16[64,8,896]{2,1,0:T(8,128)(2,1)S(1)} all-gather(bf16[2,8,896]{2,1,0:T(8,128)(2,1)S(1)} %fusion.8), channel_id=1, replica_groups=mesh['req'=32,'tp'=4] {'req'}, dimensions={0}, use_global_device_ids=true | all-gather | bytes 946176 | tf_op jit(solution)/shard_map/all_gather | solution.py:198
  121.1 23.6 %all-gather.5.cloned.1.call-done = bf16[1024,3584]{1,0:T(8,128)(2,1)} async-done(((bf16[32,3584]{1,0:T(8,128)(2,1)}), bf16[1024,3584]{1,0:T(8,128)(2,1)}) %all-gather.5.cloned.1.call-update) | async-done | bytes 7340048 | tf_op jit(solution)/shard_map/all_gather | solution.py:175
  144.7 12.1 %fusion.36 = (f32[1024]{0:T(1024)S(1)}, f32[1024,1000]{0,1:T(8,128)S(1)}) fusion(bf16[1024,3584]{1,0:T(8,128)(2,1)} %all-gather.5.cloned.1.call-done, bf16[1000,3584]{1,0:T(8,128)(2,1)} %param.29), kind=kOutput, calls=%fused_computation.70 | convolution fusion | flops 7341054976 | bytes 18608128 | tf_op jit(solution)/shard_map/dot_general | solution.py:174
  156.7 1.4 select_reduce_fusion
  158.2 24.1 %all-gather.2 = f32[32768]{0:T(1024)S(1)} all-gather(f32[1024]{0:T(1024)S(1)} %get-tuple-element.139), channel_id=4, replica_groups=mesh['req'=32,'tp'=4] {'req'}, dimensions={0}, use_global_device_ids=true | all-gather | bytes 135168 | tf_op jit(solution)/shard_map/all_gather | solution.py:14
  182.2 22.7 %all-gather = f32[32768]{0:T(1024)S(1)} all-gather(f32[1024]{0:T(1024)S(1)} %get-tuple-element.187), channel_id=2, replica_groups=mesh['req'=32,'tp'=4] {'req'}, dimensions={0}, use_global_device_ids=true | all-gather | bytes 135168 | tf_op jit(solution)/shard_map/all_gather | solution.py:14
  204.9 23.8 %all-gather.1 = f32[32768]{0:T(1024)S(1)} all-gather(f32[1024]{0:T(1024)S(1)} %get-tuple-element.140), channel_id=3, replica_groups=mesh['req'=32,'tp'=4] {'req'}, dimensions={0}, use_global_device_ids=true | all-gather | bytes 135168 | tf_op jit(solution)/shard_map/all_gather | solution.py:14
  228.9 2.8 %while.29 = (s32[]{:T(128)}, f32[1024]{0:T(1024)S(1)}, f32[1024]{0:T(1024)S(1)}, f32[1024]{0:T(1024)S(1)}, f32[31,1024]{1,0:T(8,128)S(1)}, /*index=5*/f32[31,1024]{1,0:T(8,128)S(1)}, f32[31,1024]{1,0:T(8,128)S(1)}, s32[]{:T(128)}) while((s32[]{:T(128)}, f32[1024]{0:T(1024)S(1)}, f32[1024]{0:T(1024)S(1)}, f32[1024]{0:T(1024)S(1)}, ...), condition=%wide.region_13.14_spmd, body=%wide.region_12.13_spmd.sunk | while | flops 7170 | bytes 61541 | solution.py:17
  231.7 12.5 %all_gather.40 = f32[4096]{0:T(1024)S(1)} all-gather(f32[1024]{0:T(1024)S(1)} %get-tuple-element.92), channel_id=1, replica_groups=mesh['req'=32,'tp'=4] {'tp'}, dimensions={0}, use_global_device_ids=true | all-gather | bytes 20480 | tf_op jit(solution)/shard_map/all_gather | solution.py:186
  244.2 12.0 %all_gather.41 = f32[4096]{0:T(1024)S(1)} all-gather(f32[1024]{0:T(1024)S(1)} %get-tuple-element.93), channel_id=1, replica_groups=mesh['req'=32,'tp'=4] {'tp'}, dimensions={0}, use_global_device_ids=true | all-gather | bytes 20480 | tf_op jit(solution)/shard_map/all_gather | solution.py:184
  256.2 12.0 %all_gather.42 = f32[4096]{0:T(1024)S(1)} all-gather(f32[1024]{0:T(1024)S(1)} %get-tuple-element.94), channel_id=1, replica_groups=mesh['req'=32,'tp'=4] {'tp'}, dimensions={0}, use_global_device_ids=true | all-gather | bytes 20480 | tf_op jit(solution)/shard_map/all_gather | solution.py:185
  (193 shorter events, 17.2 us)
Async XLA Ops:
  7.2 9.7 %copy-start.1 = (s32[2]{0:T(128)S(1)}, s32[2]{0:T(128)}, u32[]{:S(2)}) copy-start(s32[2]{0:T(128)} %param.24) | copy-start | bytes 28
  7.2 66.4 %reduce-scatter.4.cloned.1.call-start = ((), (), s32[]{:S(2)}) async-start(), calls=%async_computation.3 | async-start | bytes 1146880
  34.0 60.4 %copy-start = (s32[64,64]{1,0:T(8,128)S(1)}, s32[64,64]{1,0:T(8,128)}, u32[]{:S(2)}) copy-start(s32[64,64]{1,0:T(8,128)} %param.30) | copy-start | bytes 49156
  34.0 60.7 %copy-start.2 = (s32[2,8,64]{2,1,0:T(8,128)S(1)}, s32[2,8,64]{2,1,0:T(8,128)}, u32[]{:S(2)}) copy-start(s32[2,8,64]{2,1,0:T(8,128)} %param.26) | copy-start | bytes 12292
  34.0 86.2 %copy-start.3 = (s32[64]{0:T(128)S(1)}, s32[64]{0:T(128)}, u32[]{:S(2)}) copy-start(s32[64]{0:T(128)} %param.31) | copy-start | bytes 772
  35.3 109.4 %all-gather.5.cloned.1.call-start = ((), (), s32[]{:S(2)}) async-start(), calls=%async_computation.2 | async-start | bytes 7569408 | tf_op jit(solution)/shard_map/all_gather | solution.py:175
  75.7 3.6 %collective-permute-start = (f32[128]{0:T(128)S(1)}, f32[128]{0:T(128)S(1)}, u32[]{:S(2)}, u32[]{:S(2)}) collective-permute-start(f32[128]{0:T(128)S(1)} %get-tuple-element.177), channel_id=1, source_target_pairs={{0,1},{1,0},{2,3},{3,2},{4,5},{5,4},{6,7},{7,6},{8,9},{9,8},{10,11... | collective-permute-start | bytes 1544 | tf_op jit(solution)/shard_map/ppermute | solution.py:151
  79.4 5.1 %collective-permute-start.1 = (f32[128]{0:T(128)S(1)}, f32[128]{0:T(128)S(1)}, u32[]{:S(2)}, u32[]{:S(2)}) collective-permute-start(f32[128]{0:T(128)S(1)} %add.85), channel_id=1, source_target_pairs={{0,2},{1,3},{2,0},{3,1},{4,6},{5,7},{6,4},{7,5},{8,10},{9,11},{10,... | collective-permute-start | bytes 1544 | tf_op jit(solution)/shard_map/ppermute | solution.py:151
Sparse Core Ops, SparseCore 0:
  35.4 38.0 reduce-scatter.3
  94.5 50.1 all-gather.4
